TPU v7x, 32 devices: a whole 2x2x4 slice. The times are simulated.
32 devices in a mesh: slab: 4 (over x, core), chan: 2 (over y), filt: 4 (over z).
Axes of the slice: x: 2, y: 2, z: 4, core: 2. Of those that a mesh axis runs over, the one named last changes fastest.
Arguments:
- volume: bfloat16 [256, 8, 32, 128], P('chan', 'slab'), may hold values from -6 to 6
- plane_weight: bfloat16 [3, 3, 256, 256], P(None, None, 'chan', 'filt'), may hold values from -0.125 to 0.125
- depth_weight: bfloat16 [3, 256, 256], replicated, may hold values from -0.21875 to 0.21875
- grad_out: bfloat16 [256, 8, 32, 128], P('filt', 'slab', 'chan'), may hold values from -6 to 6
Outputs:
- output: bfloat16 [256, 8, 32, 128], P('filt', 'slab', 'chan')
- grad_in: bfloat16 [256, 8, 32, 128], P('chan', 'slab', 'filt')
All inputs are finite; a program needn't handle non-finite values.
Results may differ from a plain program's by a relative error of at most 0.0049.
Values may be sent and summed in bfloat16 or wider, within the bound.
No kernel may reach another device: no remote copies, remote signals or barrier semaphores. Data moves between devices by JAX's collectives and lax.ppermute only.
A program may use at most 64 MiB of HBM per device.

v0:
```python
import jax
import jax.numpy as jnp
from jax import lax
from jax.sharding import PartitionSpec as P


def with_halo(value, sides, width):
    for axis, dim in sides:
        size, length = (lax.axis_size(axis), value.shape[dim])
        up = [(i, (i + 1) % size) for i in range(size - 1)]
        down = [(j, i) for i, j in up]
        last = lax.slice_in_dim(value, length - width, length, axis=dim)
        leading = lax.slice_in_dim(value, 0, width, axis=dim)
        before = lax.ppermute(last, axis, up)
        after = lax.ppermute(leading, axis, down)
        value = jnp.concatenate([before, value, after], axis=dim)
    return value


def plane_conv(padded, weight):
    rows = padded.shape[2] - 2
    cols = padded.shape[3] - 2
    inputs = weight.shape[2]
    outputs = weight.shape[3]
    total = None
    for row_tap in range(3):
        stacked = jnp.concatenate(
            [
                padded[:, :, row_tap : row_tap + rows, col_tap : col_tap + cols]
                for col_tap in range(3)
            ],
            axis=0,
        )
        flat_weight = weight[row_tap].reshape(3 * inputs, outputs)
        term = jnp.einsum("cm,czhw->mzhw", flat_weight, stacked, preferred_element_type=jnp.float32)
        total = term if total is None else total + term
    return total


def depth_conv(padded, weight):
    depth = padded.shape[1] - 2
    stacked = jnp.stack([padded[:, tap : tap + depth] for tap in range(3)], axis=0)
    return jnp.einsum("kom,kmzhw->ozhw", weight, stacked, preferred_element_type=jnp.float32)


def pad_plane(field):
    return jnp.pad(field, ((0, 0), (0, 0), (1, 1), (1, 1)))


def pad_columns(field):
    return jnp.pad(field, ((0, 0), (0, 0), (0, 0), (1, 1)))


def local(volume, plane_weight, depth_weight, grad_out):
    filt_index = lax.axis_index("filt")
    partial_mid = plane_conv(pad_plane(volume), plane_weight)
    mid = lax.psum_scatter(partial_mid, "chan", scatter_dimension=2, tiled=True).astype(
        jnp.bfloat16
    )
    out_count = grad_out.shape[0]
    mid_count = mid.shape[0]
    forward_weight = lax.dynamic_slice_in_dim(depth_weight, filt_index * out_count, out_count, 1)
    own_columns = lax.dynamic_slice_in_dim(depth_weight, filt_index * mid_count, mid_count, 2)
    backward_weight = jnp.transpose(own_columns[::-1], (0, 2, 1))
    whole_mid = lax.all_gather(mid, "filt", axis=0, tiled=True)
    padded_mid = with_halo(whole_mid, (("slab", 1),), 1)
    output = depth_conv(padded_mid, forward_weight).astype(jnp.bfloat16)
    whole_grad = lax.all_gather(grad_out, "filt", axis=0, tiled=True)
    padded_grad = with_halo(whole_grad, (("slab", 1),), 1)
    grad_mid = depth_conv(padded_grad, backward_weight).astype(jnp.bfloat16)
    tall_grad = lax.all_gather(grad_mid, "chan", axis=2, tiled=True)
    turned = lax.all_to_all(tall_grad, "filt", split_axis=2, concat_axis=0, tiled=True)
    rimmed_grad = with_halo(turned, (("filt", 2),), 1)
    all_mid_weight = lax.all_gather(plane_weight, "filt", axis=3, tiled=True)
    flipped = jnp.transpose(all_mid_weight[::-1, ::-1], (0, 1, 3, 2))
    grad_in = plane_conv(pad_columns(rimmed_grad), flipped).astype(jnp.bfloat16)
    return (output, grad_in)


def solution(mesh):
    placed = (
        P("chan", "slab", None, None),
        P(None, None, "chan", "filt"),
        P(),
        P("filt", "slab", "chan", None),
    )
    return jax.shard_map(
        local,
        mesh=mesh,
        in_specs=placed,
        out_specs=(P("filt", "slab", "chan", None), P("chan", "slab", "filt", None)),
        check_vma=False,
    )
```

profile of v0, /device:TPU:9, one launch (start us, length us, event | category | flops | bytes accessed | tf_op | source)
XLA Modules:
  0.0 231.1 jit_solution(7157435260248938483)
XLA Ops:
  8.0 0.0 copy-start
  8.0 0.0 all-gather.6.cloned.1.call-start
  8.1 2.1 copy.65
  10.1 0.0 all-gather.6.cloned.1.call-update
  10.2 0.0 copy-start.8
  10.2 0.0 reduce-scatter.5.cloned.1.call-start
  10.2 3.0 %copy.58 = bf16[128,2,32,128]{3,0,2,1:T(8,128)(2,1)S(1)} copy(bf16[128,2,32,128]{3,2,1,0:T(8,128)(2,1)} %param.4) | data formatting | bytes 4194304 | tf_op args[0]
  13.3 0.1 reshape.4
  13.4 0.1 reshape.5
  13.5 0.1 reshape.6
  13.5 4.0 %pad_slice_fusion.2 = (bf16[128,2,32,128]{3,0,2,1:T(8,128)(2,1)S(1)}, bf16[128,2,32,128]{3,0,2,1:T(8,128)(2,1)S(1)}, bf16[128,2,32,128]{3,0,2,1:T(8,128)(2,1)S(1...) fusion(bf16[128,2,32,128]{3,0,2,1:T(8,128)(2,1)S(1)} %copy.58), kind=kLoop, calls=%fused_computation.2 | loop fusion | bytes 18874368 | tf_op jit(solution)/shard_map/slice | solution.py:29
  17.5 1.7 fusion.6
  19.2 1.7 fusion
  20.9 1.7 add_bitcast_fusion
  22.6 0.1 copy.92
  22.7 2.6 %copy.99 = f32[4,8,128,128]{3,1,2,0:T(8,128)} copy(f32[4,8,128,128]{3,2,1,0:T(8,128)S(1)} %bitcast.96) | data formatting | bytes 4194304
  25.3 0.0 reduce-scatter.5.cloned.1.call-update
  25.3 0.0 all-gather.8.cloned.1.call-start
  25.4 31.0 %all-gather.6.cloned.1.call-done = bf16[256,2,16,128]{3,0,2,1:T(8,128)(2,1)} async-done(((bf16[64,2,16,128]{3,0,2,1:T(8,128)(2,1)}), bf16[256,2,16,128]{3,0,2,1:T(8,128)(2,1)}) %all-gather.6.cloned.1.call-update) | async-done | bytes 2097168 | tf_op jit(solution)/shard_map/all_gather | solution.py:68
  56.3 2.9 %fusion.95 = (bf16[256,1,16,128]{3,0,2,1:T(8,128)(2,1)}, bf16[256,1,16,128]{3,0,2,1:T(8,128)(2,1)S(1)}) fusion(bf16[256,2,16,128]{3,0,2,1:T(8,128)(2,1)} %all-gather.6.cloned.1.call-done), kind=kLoop, calls=%fused_computation.96 | loop fusion | bytes 4194304 | tf_op jit(solution)/shard_map/slice | solution.py:12
  59.3 3.9 %collective-permute-start.2 = (bf16[256,1,16,128]{3,0,2,1:T(8,128)(2,1)}, bf16[256,1,16,128]{3,0,2,1:T(8,128)(2,1)}, u32[]{:S(2)}, u32[]{:S(2)}) collective-permute-start(bf16[256,1,16,128]{3,0,2,1:T(8,128)(2,1)} %get-tuple-element.12), channel_id=1, source_target_pairs={{0,8},{8,16},{16,24},{1,9},{9,17},{17,25},{2,10},{10,18},{18,26},{... | collective-permute-start | bytes 3145736 | tf_op jit(solution)/shard_map/ppermute | solution.py:14
  63.2 1.9 collective-permute-start.3
  65.1 0.8 constant_dynamic-slice_fusion
  65.9 1.6 rev.6
  67.5 7.7 %collective-permute-done.2 = bf16[256,1,16,128]{3,0,2,1:T(8,128)(2,1)} collective-permute-done((bf16[256,1,16,128]{3,0,2,1:T(8,128)(2,1)}, bf16[256,1,16,128]{3,0,2,1:T(8,128)(2,1)}, u32[]{:S(2)}, u32[]{:S(2)}) %collective-permute-start.2) | collective-permute-done | bytes 1048608 | tf_op jit(solution)/shard_map/ppermute | solution.py:14
  75.2 4.2 %collective-permute-done.3 = bf16[256,1,16,128]{3,0,2,1:T(8,128)(2,1)} collective-permute-done((bf16[256,1,16,128]{3,0,2,1:T(8,128)(2,1)S(1)}, bf16[256,1,16,128]{3,0,2,1:T(8,128)(2,1)}, u32[]{:S(2)}, u32[]{:S(2)}) %collective-permute-start.3) | collective-permute-done | bytes 1048608 | tf_op jit(solution)/shard_map/ppermute | solution.py:15
  79.4 1.9 fusion.46
  81.3 2.1 fusion.74
  83.4 0.0 all-gather.8.cloned.1.call-update
  83.5 0.0 all-gather.4.cloned.1.call-start
  83.5 0.0 reduce-scatter.5.cloned.1.call-done
  83.5 1.4 copy.95
  85.0 0.8 copy.98
  85.8 0.0 all-gather.4.cloned.1.call-update
  85.8 0.0 copy-start.9
  85.8 17.6 %all-gather.8.cloned.1.call-done = bf16[64,2,32,128]{3,0,2,1:T(8,128)(2,1)} async-done(((bf16[64,2,16,128]{3,0,2,1:T(8,128)(2,1)}), bf16[64,2,32,128]{3,0,2,1:T(8,128)(2,1)}) %all-gather.8.cloned.1.call-update) | async-done | bytes 1048592 | tf_op jit(solution)/shard_map/all_gather | solution.py:71
  103.5 2.3 copy.69
  105.8 4.6 %all-to-all-start = ((bf16[64,2,32,128]{3,0,1,2:T(8,128)(2,1)}), bf16[64,2,32,128]{3,0,1,2:T(8,128)(2,1)S(1)}, u32[]{:S(2)}, u32[]{:S(2)}) async-start(bf16[64,2,32,128]{3,0,1,2:T(8,128)(2,1)} %copy.69), calls=%async_computation | async-start | bytes 2097152 | tf_op jit(solution)/shard_map/all_to_all | solution.py:72
  110.4 64.2 %all_gather.15 = bf16[3,3,128,256]{2,3,1,0:T(8,128)(2,1)S(1)} all-gather(bf16[3,3,128,64]{2,3,1,0:T(8,128)(2,1)S(1)} %copy-done.9), channel_id=1, replica_groups=mesh['slab'=4,'chan'=2,'filt'=4] {'filt'}, dimensions={3}, use_global_device_ids=true | all-gather | bytes 737280 | tf_op jit(solution)/shard_map/all_gather | solution.py:74
  174.6 0.9 reverse_bitcast_fusion
  175.5 0.7 copy.71
  176.1 0.8 copy.72
  177.0 1.9 collective-permute-start.5
  178.9 3.4 %collective-permute-start.4 = (bf16[256,2,1,128]{0,3,2,1:T(8,128)(2,1)S(1)}, bf16[256,2,1,128]{0,3,2,1:T(8,128)(2,1)S(1)}, u32[]{:S(2)}, u32[]{:S(2)}) collective-permute-start(bf16[256,2,1,128]{0,3,2,1:T(8,128)(2,1)S(1)} %get-tuple-element.32), channel_id=1, source_target_pairs={{0,1},{1,2},{2,3},{4,5},{5,6},{6,7},{8,9},{9,10},{10,11},{12,13},{... | collective-permute-start | bytes 393224 | tf_op jit(solution)/shard_map/ppermute | solution.py:14
  182.3 0.8 fusion.99
  183.1 1.5 collective-permute-done.4
  184.6 0.7 copy-done.14
  185.3 0.7 fusion.55
  186.0 3.2 %fusion.97 = (bf16[256,2,8,128]{0,3,2,1:T(8,128)(2,1)}, bf16[256,2,8,128]{0,3,2,1:T(8,128)(2,1)S(1)}, bf16[256,2,8,128]{0,3,2,1:T(8,128)(2,1)}, bf16[256,2,8,128...) fusion(bf16[256,2,10,130]{0,3,2,1:T(8,128)(2,1)S(1)} %fusion.55), kind=kLoop, calls=%fused_computation.98 | loop fusion | bytes 12582912 | tf_op jit(solution)/shard_map/slice | solution.py:29
  189.2 3.3 %fusion.96 = (bf16[256,1,16,128]{3,0,2,1:T(8,128)(2,1)}, bf16[256,1,16,128]{3,0,2,1:T(8,128)(2,1)}) fusion(bf16[256,2,16,128]{3,0,2,1:T(8,128)(2,1)} %all-gather.4.cloned.1.call-done), kind=kLoop, calls=%fused_computation.97 | loop fusion | bytes 4194304 | tf_op jit(solution)/shard_map/slice | solution.py:12
  192.5 10.1 %collective-permute-start = (bf16[256,1,16,128]{3,0,2,1:T(8,128)(2,1)}, bf16[256,1,16,128]{3,0,2,1:T(8,128)(2,1)}, u32[]{:S(2)}, u32[]{:S(2)}) collective-permute-start(bf16[256,1,16,128]{3,0,2,1:T(8,128)(2,1)} %get-tuple-element.16), channel_id=1, source_target_pairs={{0,8},{8,16},{16,24},{1,9},{9,17},{17,25},{2,10},{10,18},{18,26},{... | collective-permute-start | bytes 3145736 | tf_op jit(solution)/shard_map/ppermute | solution.py:14
  202.6 2.1 collective-permute-start.1
  204.8 1.2 fusion.34
  206.0 1.2 fusion.42
  207.2 0.3 copy-done.5
  207.5 0.0 copy-done.10
  207.5 0.0 copy-done.15
  207.6 1.9 fusion.77
  209.5 2.2 copy.79
  211.7 2.9 %collective-permute-done = bf16[256,1,16,128]{3,0,2,1:T(8,128)(2,1)} collective-permute-done((bf16[256,1,16,128]{3,0,2,1:T(8,128)(2,1)}, bf16[256,1,16,128]{3,0,2,1:T(8,128)(2,1)}, u32[]{:S(2)}, u32[]{:S(2)}) %collective-permute-start) | collective-permute-done | bytes 1048608 | tf_op jit(solution)/shard_map/ppermute | solution.py:14
  214.7 4.4 %collective-permute-done.1 = bf16[256,1,16,128]{3,0,2,1:T(8,128)(2,1)} collective-permute-done((bf16[256,1,16,128]{3,0,2,1:T(8,128)(2,1)}, bf16[256,1,16,128]{3,0,2,1:T(8,128)(2,1)}, u32[]{:S(2)}, u32[]{:S(2)}) %collective-permute-start.1) | collective-permute-done | bytes 1048608 | tf_op jit(solution)/shard_map/ppermute | solution.py:15
  219.1 1.9 fusion.48
  221.0 1.4 fusion.71
  222.4 1.1 copy.78
  (37 shorter events, 0.2 us)
Async XLA Ops:
  8.0 57.1 %copy-start = (bf16[3,256,256]{2,1,0:T(8,128)(2,1)S(1)}, bf16[3,256,256]{2,1,0:T(8,128)(2,1)}, u32[]{:S(2)}) copy-start(bf16[3,256,256]{2,1,0:T(8,128)(2,1)} %param.6) | copy-start | bytes 1179652
  8.0 48.3 %all-gather.6.cloned.1.call-start = ((), (), s32[]{:S(2)}) async-start(), calls=%async_computation.3 | async-start | bytes 2621440 | tf_op jit(solution)/shard_map/all_gather | solution.py:68
  10.2 3.0 %copy-start.8 = (bf16[3,3,128,64]{2,3,1,0:T(8,128)(2,1)S(1)}, bf16[3,3,128,64]{2,3,1,0:T(8,128)(2,1)}, u32[]{:S(2)}) copy-start(bf16[3,3,128,64]{2,3,1,0:T(8,128)(2,1)} %param.5) | copy-start | bytes 442372
  10.2 73.4 %reduce-scatter.5.cloned.1.call-start = ((), (), s32[]{:S(2)}) async-start(), calls=%async_computation.5 | async-start | bytes 3145728
  25.3 78.2 %all-gather.8.cloned.1.call-start = ((), (), s32[]{:S(2)}) async-start(), calls=%async_computation.4 | async-start | bytes 1572864 | tf_op jit(solution)/shard_map/all_gather | solution.py:71
  56.3 23.1 %copy-start.1 = (bf16[256,2,16,128]{3,0,2,1:T(8,128)(2,1)S(1)}, bf16[256,2,16,128]{3,0,2,1:T(8,128)(2,1)}, u32[]{:S(2)}) copy-start(bf16[256,2,16,128]{3,0,2,1:T(8,128)(2,1)} %all-gather.6.cloned.1.call-done) | copy-start | bytes 6291460
  59.3 15.9 %collective-permute-start.2 = (bf16[256,1,16,128]{3,0,2,1:T(8,128)(2,1)}, bf16[256,1,16,128]{3,0,2,1:T(8,128)(2,1)}, u32[]{:S(2)}, u32[]{:S(2)}) collective-permute-start(bf16[256,1,16,128]{3,0,2,1:T(8,128)(2,1)} %get-tuple-element.12), channel_id=1, source_target_pairs={{0,8},{8,16},{16,24},{1,9},{9,17},{17,25},{2,10},{10,18},{18,26},{... | collective-permute-start | bytes 3145736 | tf_op jit(solution)/shard_map/ppermute | solution.py:14
  63.2 16.2 %collective-permute-start.3 = (bf16[256,1,16,128]{3,0,2,1:T(8,128)(2,1)S(1)}, bf16[256,1,16,128]{3,0,2,1:T(8,128)(2,1)}, u32[]{:S(2)}, u32[]{:S(2)}) collective-permute-start(bf16[256,1,16,128]{3,0,2,1:T(8,128)(2,1)S(1)} %get-tuple-element.13), channel_id=1, source_target_pairs={{8,0},{16,8},{24,16},{9,1},{17,9},{25,17},{10,2},{18,10},{26,18},{... | collective-permute-start | bytes 3145736 | tf_op jit(solution)/shard_map/ppermute | solution.py:15
  67.5 13.8 %copy-start.13 = (bf16[3,256,64]{2,1,0:T(8,128)(2,1)S(1)}, bf16[3,256,64]{2,1,0:T(8,128)(2,1)}, u32[]{:S(2)}) copy-start(bf16[3,256,64]{2,1,0:T(8,128)(2,1)} %rev.6) | copy-start | bytes 294916
  83.5 105.7 %all-gather.4.cloned.1.call-start = ((), (), s32[]{:S(2)}) async-start(), calls=%async_computation.2 | async-start | bytes 2621440 | tf_op jit(solution)/shard_map/all_gather | solution.py:65
  85.8 24.5 %copy-start.9 = (bf16[3,3,128,64]{2,3,1,0:T(8,128)(2,1)S(1)}, bf16[3,3,128,64]{2,3,1,0:T(8,128)(2,1)}, u32[]{:S(2)}) copy-start(bf16[3,3,128,64]{2,3,1,0:T(8,128)(2,1)} %param.5) | copy-start | bytes 442372
  105.8 69.7 %all-to-all-start = ((bf16[64,2,32,128]{3,0,1,2:T(8,128)(2,1)}), bf16[64,2,32,128]{3,0,1,2:T(8,128)(2,1)S(1)}, u32[]{:S(2)}, u32[]{:S(2)}) async-start(bf16[64,2,32,128]{3,0,1,2:T(8,128)(2,1)} %copy.69), calls=%async_computation | async-start | bytes 2097152 | tf_op jit(solution)/shard_map/all_to_all | solution.py:72
  176.1 6.1 %copy-start.3 = (bf16[3,3,256,128]{3,2,1,0:T(8,128)(2,1)S(1)}, bf16[3,3,256,128]{3,2,1,0:T(8,128)(2,1)}, u32[]{:S(2)}) copy-start(bf16[3,3,256,128]{3,2,1,0:T(8,128)(2,1)} %reverse_bitcast_fusion) | copy-start | bytes 1769476
  177.0 6.1 %collective-permute-start.5 = (bf16[256,2,1,128]{0,3,2,1:T(8,128)(2,1)S(1)}, bf16[256,2,1,128]{0,3,2,1:T(8,128)(2,1)S(1)}, u32[]{:S(2)}, u32[]{:S(2)}) collective-permute-start(bf16[256,2,1,128]{0,3,2,1:T(8,128)(2,1)S(1)} %get-tuple-element.33), channel_id=1, source_target_pairs={{1,0},{2,1},{3,2},{5,4},{6,5},{7,6},{9,8},{10,9},{11,10},{13,12},{... | collective-permute-start | bytes 393224 | tf_op jit(solution)/shard_map/ppermute | solution.py:15
  178.9 5.7 %collective-permute-start.4 = (bf16[256,2,1,128]{0,3,2,1:T(8,128)(2,1)S(1)}, bf16[256,2,1,128]{0,3,2,1:T(8,128)(2,1)S(1)}, u32[]{:S(2)}, u32[]{:S(2)}) collective-permute-start(bf16[256,2,1,128]{0,3,2,1:T(8,128)(2,1)S(1)} %get-tuple-element.32), channel_id=1, source_target_pairs={{0,1},{1,2},{2,3},{4,5},{5,6},{6,7},{8,9},{9,10},{10,11},{12,13},{... | collective-permute-start | bytes 393224 | tf_op jit(solution)/shard_map/ppermute | solution.py:14
  183.1 1.5 copy-start.16
  184.6 0.7 copy-start.14
  189.2 15.6 %copy-start.6 = (bf16[256,2,8,128]{0,3,2,1:T(8,128)(2,1)S(1)}, bf16[256,2,8,128]{0,3,2,1:T(8,128)(2,1)}, u32[]{:S(2)}) copy-start(bf16[256,2,8,128]{0,3,2,1:T(8,128)(2,1)} %get-tuple-element.28) | copy-start | bytes 3145732
  189.2 15.6 %copy-start.7 = (bf16[256,2,8,128]{0,3,2,1:T(8,128)(2,1)S(1)}, bf16[256,2,8,128]{0,3,2,1:T(8,128)(2,1)}, u32[]{:S(2)}) copy-start(bf16[256,2,8,128]{0,3,2,1:T(8,128)(2,1)} %get-tuple-element.29) | copy-start | bytes 3145732
  189.2 15.6 %copy-start.12 = (bf16[1,3,256,128]{3,2,1,0:T(8,128)(2,1)S(1)}, bf16[1,3,256,128]{3,2,1,0:T(8,128)(2,1)}, u32[]{:S(2)}) copy-start(bf16[1,3,256,128]{3,2,1,0:T(8,128)(2,1)} %get-tuple-element.36) | copy-start | bytes 589828
  192.5 22.2 %collective-permute-start = (bf16[256,1,16,128]{3,0,2,1:T(8,128)(2,1)}, bf16[256,1,16,128]{3,0,2,1:T(8,128)(2,1)}, u32[]{:S(2)}, u32[]{:S(2)}) collective-permute-start(bf16[256,1,16,128]{3,0,2,1:T(8,128)(2,1)} %get-tuple-element.16), channel_id=1, source_target_pairs={{0,8},{8,16},{16,24},{1,9},{9,17},{17,25},{2,10},{10,18},{18,26},{... | collective-permute-start | bytes 3145736 | tf_op jit(solution)/shard_map/ppermute | solution.py:14
  202.6 16.4 %collective-permute-start.1 = (bf16[256,1,16,128]{3,0,2,1:T(8,128)(2,1)}, bf16[256,1,16,128]{3,0,2,1:T(8,128)(2,1)}, u32[]{:S(2)}, u32[]{:S(2)}) collective-permute-start(bf16[256,1,16,128]{3,0,2,1:T(8,128)(2,1)} %get-tuple-element.17), channel_id=1, source_target_pairs={{8,0},{16,8},{24,16},{9,1},{17,9},{25,17},{10,2},{18,10},{26,18},{... | collective-permute-start | bytes 3145736 | tf_op jit(solution)/shard_map/ppermute | solution.py:15
  204.8 1.2 copy-start.11
  204.8 1.2 copy-start.17
  206.0 1.2 copy-start.4
  206.0 1.5 copy-start.5
  206.0 1.5 copy-start.10
  206.0 1.6 copy-start.15
  207.6 11.5 %copy-start.2 = (bf16[256,2,16,128]{3,0,2,1:T(8,128)(2,1)S(1)}, bf16[256,2,16,128]{3,0,2,1:T(8,128)(2,1)}, u32[]{:S(2)}) copy-start(bf16[256,2,16,128]{3,0,2,1:T(8,128)(2,1)} %all-gather.4.cloned.1.call-done) | copy-start | bytes 6291460
Sparse Core Ops, SparseCore 0:
  11.1 45.2 all-gather.5
Sparse Core Ops, SparseCore 1:
  25.4 32.8 reduce-scatter.4
  83.5 19.9 all-gather.7
  105.6 70.7 all-gather.3
where the time goes:
time: 232 us; the launch traced here: 231 us
  waiting for transfers between devices  69.4 us (30%)
  blocking collectives  64.2 us (28%)
  local copies, waits for them, and re-layouts  36.1 us (16%)
  starting transfers between devices  28.1 us (12%)
  between operations  16 us (7%)
  matrix products  12.8 us (6%)
  other arithmetic  4.51 us (2%)
    all_gather x1, blocking collectives, local(): all_mid_weight = lax.all_gather(plane_weight, 'filt', axis=3, tiled=True)  64.2 us
    all_gather x1, waiting for transfers between devices, local(): whole_grad = lax.all_gather(grad_out, 'filt', axis=0, tiled=True)  31 us
    all_gather x1, waiting for transfers between devices, local(): tall_grad = lax.all_gather(grad_mid, 'chan', axis=2, tiled=True)  17.6 us
    ppermute x3, starting transfers between devices, with_halo(): before = lax.ppermute(last, axis, up)  17.4 us
    unnamed x44, local copies, waits for them, and re-layouts  14.5 us
    ppermute x3, waiting for transfers between devices, with_halo(): before = lax.ppermute(last, axis, up)  12.1 us
    dot_general x6, matrix products, plane_conv(): jnp.einsum('cm,czhw->mzhw', flat_weight, stacked, preferred_element_type=...  9.31 us
    ppermute x3, waiting for transfers between devices, with_halo(): after = lax.ppermute(leading, axis, down)  8.59 us
  transfers between devices with their start and end apart: 11, of which 7 were waited for; matrix products, arithmetic and copies ran while one was open for 18% of the time, Pallas kernels for 0%

commit v1 on v0

--- a/solution.py
+++ b/solution.py
@@ -2,6 +2,39 @@
 import jax.numpy as jnp
 from jax import lax
 from jax.sharding import PartitionSpec as P
+
+
+def _get_steps_all(here_x, array_axis, payload):
+    new = here_x.shape
+    inter = here_x.reshape(
+        *new[:array_axis], payload, new[array_axis] // payload, *new[array_axis + 1 :]
+    )
+    return jnp.moveaxis(inter, array_axis, 0)
+
+
+def _supply_ports(vector, along_dim):
+    vector = jnp.moveaxis(vector, 0, along_dim)
+    near = vector.shape
+    return vector.reshape(
+        *near[:along_dim], near[along_dim] * near[along_dim + 1], *near[along_dim + 2 :]
+    )
+
+
+def _plan_rails(local_x, mesh_ax, target, mat):
+    f_next = lax.axis_size(mesh_ax)
+    kept_arr = lax.axis_index(mesh_ax)
+    a_next, state_next = (f_next, kept_arr)
+    m_next = _get_steps_all(local_x, target, a_next)
+    by_rank = [m_next[state_next]]
+    for hop_no in [*range(1, a_next)]:
+        right_arr = m_next[state_next ^ hop_no]
+        b_now = lax.ppermute(
+            right_arr, axis_name=mesh_ax, perm=[(dev_j, dev_j ^ hop_no) for dev_j in range(a_next)]
+        )
+        by_rank.append(b_now)
+    k_now = jnp.stack(by_rank, axis=0)
+    m_next = k_now[state_next ^ jnp.arange(a_next)]
+    return _supply_ports(m_next, mat)
 
 
 def with_halo(value, sides, width):
@@ -69,7 +102,7 @@
     padded_grad = with_halo(whole_grad, (("slab", 1),), 1)
     grad_mid = depth_conv(padded_grad, backward_weight).astype(jnp.bfloat16)
     tall_grad = lax.all_gather(grad_mid, "chan", axis=2, tiled=True)
-    turned = lax.all_to_all(tall_grad, "filt", split_axis=2, concat_axis=0, tiled=True)
+    turned = _plan_rails(tall_grad, "filt", 2, 0)
     rimmed_grad = with_halo(turned, (("filt", 2),), 1)
     all_mid_weight = lax.all_gather(plane_weight, "filt", axis=3, tiled=True)
     flipped = jnp.transpose(all_mid_weight[::-1, ::-1], (0, 1, 3, 2))

time: 232 us -> 211 us (0.909)
  blocking collectives: 64.2 us -> 11.9 us
  waiting for transfers between devices: 69.4 us -> 95.6 us
  starting transfers between devices: 28.1 us -> 32.7 us
    all_gather x1, blocking collectives: 64.2 us -> 11.9 us  [local(): all_mid_weight = lax.all_gather(plane_weight, 'filt', axis=3, tiled=True)]
    ppermute x0 -> x3, waiting for transfers between devices: none -> 35.6 us  [_plan_rails(): lax.ppermute(right_arr, axis_name=mesh_ax, perm=[(dev_j, dev_j ^ hop_no)...]
    all_gather x1, waiting for transfers between devices: 17.6 us -> 5.76 us  [local(): tall_grad = lax.all_gather(grad_mid, 'chan', axis=2, tiled=True)]
    ppermute x3, starting transfers between devices: 5.94 us -> 14.4 us  [with_halo(): after = lax.ppermute(leading, axis, down)]
    all_to_all x1 -> x0, starting transfers between devices: 4.57 us -> none  [local(): lax.all_to_all(tall_grad, 'filt', split_axis=2, concat_axis=0, tiled=True)]
    ppermute x0 -> x3, starting transfers between devices: none -> 3.52 us  [_plan_rails(): lax.ppermute(right_arr, axis_name=mesh_ax, perm=[(dev_j, dev_j ^ hop_no)...]
    ppermute x3, starting transfers between devices: 17.4 us -> 14.6 us  [with_halo(): before = lax.ppermute(last, axis, up)]
  transfers between devices with their start and end apart: 11 -> 13, of which waited for: 7 -> 10; matrix products, arithmetic and copies ran while one was open for 18% -> 20% of each run, Pallas kernels for 0% -> 0%
where the time goes in v1:
time: 211 us; the launch traced here: 209 us
  waiting for transfers between devices  95.6 us (45%)
  local copies, waits for them, and re-layouts  35.7 us (17%)
  starting transfers between devices  32.7 us (15%)
  between operations  16.1 us (8%)
  matrix products  12.8 us (6%)
  blocking collectives  11.9 us (6%)
  other arithmetic  4.65 us (2%)
    ppermute x3, waiting for transfers between devices, _plan_rails(): lax.ppermute(right_arr, axis_name=mesh_ax, perm=[(dev_j, dev_j ^ hop_no)...  35.6 us
    all_gather x1, waiting for transfers between devices, local(): whole_grad = lax.all_gather(grad_out, 'filt', axis=0, tiled=True)  31 us
    ppermute x3, starting transfers between devices, with_halo(): before = lax.ppermute(last, axis, up)  14.6 us
    unnamed x44, local copies, waits for them, and re-layouts  14.5 us
    ppermute x3, starting transfers between devices, with_halo(): after = lax.ppermute(leading, axis, down)  14.4 us
    ppermute x3, waiting for transfers between devices, with_halo(): before = lax.ppermute(last, axis, up)  13 us
    all_gather x1, blocking collectives, local(): all_mid_weight = lax.all_gather(plane_weight, 'filt', axis=3, tiled=True)  11.9 us
    ppermute x3, waiting for transfers between devices, with_halo(): after = lax.ppermute(leading, axis, down)  10.2 us
  transfers between devices with their start and end apart: 13, of which 10 were waited for; matrix products, arithmetic and copies ran while one was open for 20% of the time, Pallas kernels for 0%

profile of v1, /device:TPU:9, one launch (start us, length us, event | category | flops | bytes accessed | tf_op | source)
XLA Modules:
  0.0 209.5 jit_solution(17764982691289297933)
XLA Ops:
  8.0 0.0 all-gather.6.cloned.1.call-start
  8.1 2.1 copy.47
  10.2 0.0 reduce-scatter.5.cloned.1.call-start
  10.2 3.0 %copy.40 = bf16[128,2,32,128]{3,0,2,1:T(8,128)(2,1)S(1)} copy(bf16[128,2,32,128]{3,2,1,0:T(8,128)(2,1)} %param.4) | data formatting | bytes 4194304 | tf_op args[0]
  13.3 0.1 reshape.43
  13.4 0.1 reshape.44
  13.5 0.1 reshape.45
  13.5 4.0 %pad_slice_fusion.2 = (bf16[128,2,32,128]{3,0,2,1:T(8,128)(2,1)S(1)}, bf16[128,2,32,128]{3,0,2,1:T(8,128)(2,1)S(1)}, bf16[128,2,32,128]{3,0,2,1:T(8,128)(2,1)S(1...) fusion(bf16[128,2,32,128]{3,0,2,1:T(8,128)(2,1)S(1)} %copy.40), kind=kLoop, calls=%fused_computation.3 | loop fusion | bytes 18874368 | tf_op jit(solution)/shard_map/slice | solution.py:62
  17.5 1.7 fusion.6
  19.2 1.7 fusion
  20.9 1.7 add_bitcast_fusion
  22.6 0.1 copy.74
  22.7 2.6 %copy.85 = f32[4,8,128,128]{3,1,2,0:T(8,128)} copy(f32[4,8,128,128]{3,2,1,0:T(8,128)S(1)} %bitcast.111) | data formatting | bytes 4194304
  25.3 0.0 all-gather.8.cloned.1.call-start
  25.4 31.0 %all-gather.6.cloned.1.call-done = bf16[256,2,16,128]{3,0,2,1:T(8,128)(2,1)} async-done(((bf16[64,2,16,128]{3,0,2,1:T(8,128)(2,1)}), bf16[256,2,16,128]{3,0,2,1:T(8,128)(2,1)}) %all-gather.6.cloned.1.call-update) | async-done | bytes 2097168 | tf_op jit(solution)/shard_map/all_gather | solution.py:101
  56.3 2.9 %fusion.96 = (bf16[256,1,16,128]{3,0,2,1:T(8,128)(2,1)}, bf16[256,1,16,128]{3,0,2,1:T(8,128)(2,1)S(1)}) fusion(bf16[256,2,16,128]{3,0,2,1:T(8,128)(2,1)} %all-gather.6.cloned.1.call-done), kind=kLoop, calls=%fused_computation.109 | loop fusion | bytes 4194304 | tf_op jit(solution)/shard_map/slice | solution.py:45
  59.3 3.9 %collective-permute-start.2 = (bf16[256,1,16,128]{3,0,2,1:T(8,128)(2,1)}, bf16[256,1,16,128]{3,0,2,1:T(8,128)(2,1)}, u32[]{:S(2)}, u32[]{:S(2)}) collective-permute-start(bf16[256,1,16,128]{3,0,2,1:T(8,128)(2,1)} %get-tuple-element.10), channel_id=1, source_target_pairs={{0,8},{8,16},{16,24},{1,9},{9,17},{17,25},{2,10},{10,18},{18,26},{... | collective-permute-start | bytes 3145736 | tf_op jit(solution)/shard_map/ppermute | solution.py:47
  63.2 1.9 collective-permute-start.3
  65.1 0.8 constant_dynamic-slice_fusion.4
  65.9 1.6 rev.6
  67.5 7.7 %collective-permute-done.2 = bf16[256,1,16,128]{3,0,2,1:T(8,128)(2,1)} collective-permute-done((bf16[256,1,16,128]{3,0,2,1:T(8,128)(2,1)}, bf16[256,1,16,128]{3,0,2,1:T(8,128)(2,1)}, u32[]{:S(2)}, u32[]{:S(2)}) %collective-permute-start.2) | collective-permute-done | bytes 1048608 | tf_op jit(solution)/shard_map/ppermute | solution.py:47
  75.2 4.4 %collective-permute-done.3 = bf16[256,1,16,128]{3,0,2,1:T(8,128)(2,1)} collective-permute-done((bf16[256,1,16,128]{3,0,2,1:T(8,128)(2,1)S(1)}, bf16[256,1,16,128]{3,0,2,1:T(8,128)(2,1)}, u32[]{:S(2)}, u32[]{:S(2)}) %collective-permute-start.3) | collective-permute-done | bytes 1048608 | tf_op jit(solution)/shard_map/ppermute | solution.py:48
  79.6 1.9 fusion.46
  81.5 2.1 %fusion.74 = bf16[64,2,16,128]{3,0,2,1:T(8,128)(2,1)} fusion(bf16[1,256,2,16,128]{4,1,0,3,2:T(8,128)(2,1)S(1)} %get-tuple-element.9, bf16[1,256,2,16,128]{4,1,0,3,2:T(8,128)(2,1)S(1)} %bitcast.113, bf16[1,256,2,16,128]{4,1,0,3,2:T(8,128)(2,1)S(1)} %get-tuple-element.8, bf16[3,256,64]{2,1,0:T(8,128)(2,1)S(1)} %copy-done.13), kind=kOutput, calls=%fused_computation.77 | convolution fusion | flops 421789696 | bytes 6914048 | tf_op jit(solution)/shard_map/kom,kmzhw->ozhw/dot_general | solution.py:76
  83.6 0.0 all-gather.4.cloned.1.call-start
  83.7 1.4 copy.77
  85.1 0.8 copy.84
  86.0 11.9 %all_gather.15 = bf16[3,3,128,256]{2,3,1,0:T(8,128)(2,1)S(1)} all-gather(bf16[3,3,128,64]{2,3,1,0:T(8,128)(2,1)S(1)} %copy-done.9), channel_id=1, replica_groups=mesh['slab'=4,'chan'=2,'filt'=4] {'filt'}, dimensions={3}, use_global_device_ids=true | all-gather | bytes 737280 | tf_op jit(solution)/shard_map/all_gather | solution.py:107
  97.9 5.8 %all-gather.8.cloned.1.call-done = bf16[64,2,32,128]{3,0,2,1:T(8,128)(2,1)} async-done(((bf16[64,2,16,128]{3,0,2,1:T(8,128)(2,1)}), bf16[64,2,32,128]{3,0,2,1:T(8,128)(2,1)}) %all-gather.8.cloned.1.call-update) | async-done | bytes 1048592 | tf_op jit(solution)/shard_map/all_gather | solution.py:104
  103.7 1.3 constant_dynamic-slice_fusion.3
  104.9 0.2 copy.86
  105.1 1.3 collective-permute-start.6
  106.4 0.2 copy.87
  106.5 1.2 collective-permute-start.5
  107.7 0.2 copy.88
  107.9 1.1 collective-permute-start.4
  109.0 0.9 reverse_bitcast_fusion
  109.9 0.2 copy.89
  110.0 21.6 %collective-permute-done.6 = bf16[64,2,8,128]{3,2,1,0:T(8,128)(2,1)S(1)} collective-permute-done((bf16[64,2,8,128]{3,2,1,0:T(8,128)(2,1)S(1)}, bf16[64,2,8,128]{3,2,1,0:T(8,128)(2,1)S(1)}, u32[]{:S(2)}, u32[]{:S(2)}) %collective-permute-start.6) | collective-permute-done | bytes 262176 | tf_op jit(solution)/shard_map/ppermute | solution.py:31
  131.6 14.0 %collective-permute-done.5 = bf16[64,2,8,128]{3,2,1,0:T(8,128)(2,1)S(1)} collective-permute-done((bf16[64,2,8,128]{3,2,1,0:T(8,128)(2,1)S(1)}, bf16[64,2,8,128]{3,2,1,0:T(8,128)(2,1)S(1)}, u32[]{:S(2)}, u32[]{:S(2)}) %collective-permute-start.5) | collective-permute-done | bytes 262176 | tf_op jit(solution)/shard_map/ppermute | solution.py:31
  145.6 0.1 pad_maximum_fusion.6
  145.7 0.7 gather_fusion
  146.5 0.8 copy.55
  147.3 10.4 %collective-permute-start.8 = (bf16[256,2,1,128]{0,3,2,1:T(8,128)(2,1)S(1)}, bf16[256,2,1,128]{0,3,2,1:T(8,128)(2,1)S(1)}, u32[]{:S(2)}, u32[]{:S(2)}) collective-permute-start(bf16[256,2,1,128]{0,3,2,1:T(8,128)(2,1)S(1)} %get-tuple-element.31), channel_id=1, source_target_pairs={{1,0},{2,1},{3,2},{5,4},{6,5},{7,6},{9,8},{10,9},{11,10},{13,12},{... | collective-permute-start | bytes 393224 | tf_op jit(solution)/shard_map/ppermute | solution.py:48
  157.8 1.9 collective-permute-start.7
  159.7 0.8 fusion.100
  160.5 1.4 collective-permute-done.8
  161.9 2.4 %collective-permute-done.7 = bf16[256,2,1,128]{0,3,2,1:T(8,128)(2,1)S(1)} collective-permute-done((bf16[256,2,1,128]{0,3,2,1:T(8,128)(2,1)S(1)}, bf16[256,2,1,128]{0,3,2,1:T(8,128)(2,1)S(1)}, u32[]{:S(2)}, u32[]{:S(2)}) %collective-permute-start.7) | collective-permute-done | bytes 131104 | tf_op jit(solution)/shard_map/ppermute | solution.py:47
  164.4 0.7 copy-done.14
  165.0 0.7 fusion.55
  165.7 3.2 %fusion.98 = (bf16[256,2,8,128]{0,3,2,1:T(8,128)(2,1)}, bf16[256,2,8,128]{0,3,2,1:T(8,128)(2,1)S(1)}, bf16[256,2,8,128]{0,3,2,1:T(8,128)(2,1)}, bf16[256,2,8,128...) fusion(bf16[256,2,10,130]{0,3,2,1:T(8,128)(2,1)S(1)} %fusion.55), kind=kLoop, calls=%fused_computation.111 | loop fusion | bytes 12582912 | tf_op jit(solution)/shard_map/slice | solution.py:62
  168.9 3.3 %fusion.97 = (bf16[256,1,16,128]{3,0,2,1:T(8,128)(2,1)}, bf16[256,1,16,128]{3,0,2,1:T(8,128)(2,1)}) fusion(bf16[256,2,16,128]{3,0,2,1:T(8,128)(2,1)} %all-gather.4.cloned.1.call-done), kind=kLoop, calls=%fused_computation.110 | loop fusion | bytes 4194304 | tf_op jit(solution)/shard_map/slice | solution.py:45
  172.2 8.8 %collective-permute-start = (bf16[256,1,16,128]{3,0,2,1:T(8,128)(2,1)}, bf16[256,1,16,128]{3,0,2,1:T(8,128)(2,1)}, u32[]{:S(2)}, u32[]{:S(2)}) collective-permute-start(bf16[256,1,16,128]{3,0,2,1:T(8,128)(2,1)} %get-tuple-element.14), channel_id=1, source_target_pairs={{0,8},{8,16},{16,24},{1,9},{9,17},{17,25},{2,10},{10,18},{18,26},{... | collective-permute-start | bytes 3145736 | tf_op jit(solution)/shard_map/ppermute | solution.py:47
  181.0 2.1 %collective-permute-start.1 = (bf16[256,1,16,128]{3,0,2,1:T(8,128)(2,1)}, bf16[256,1,16,128]{3,0,2,1:T(8,128)(2,1)}, u32[]{:S(2)}, u32[]{:S(2)}) collective-permute-start(bf16[256,1,16,128]{3,0,2,1:T(8,128)(2,1)} %get-tuple-element.15), channel_id=1, source_target_pairs={{8,0},{16,8},{24,16},{9,1},{17,9},{25,17},{10,2},{18,10},{26,18},{... | collective-permute-start | bytes 3145736 | tf_op jit(solution)/shard_map/ppermute | solution.py:48
  183.2 1.2 fusion.34
  184.4 1.2 fusion.42
  185.6 0.3 copy-done.5
  186.0 1.9 fusion.77
  187.9 2.2 %copy.62 = bf16[128,2,8,128]{3,2,1,0:T(8,128)(2,1)} copy(bf16[128,2,8,128]{0,3,2,1:T(8,128)(2,1)} %fusion.77) | data formatting | bytes 1048576
  190.1 2.9 %collective-permute-done = bf16[256,1,16,128]{3,0,2,1:T(8,128)(2,1)} collective-permute-done((bf16[256,1,16,128]{3,0,2,1:T(8,128)(2,1)}, bf16[256,1,16,128]{3,0,2,1:T(8,128)(2,1)}, u32[]{:S(2)}, u32[]{:S(2)}) %collective-permute-start) | collective-permute-done | bytes 1048608 | tf_op jit(solution)/shard_map/ppermute | solution.py:47
  193.0 4.4 %collective-permute-done.1 = bf16[256,1,16,128]{3,0,2,1:T(8,128)(2,1)} collective-permute-done((bf16[256,1,16,128]{3,0,2,1:T(8,128)(2,1)}, bf16[256,1,16,128]{3,0,2,1:T(8,128)(2,1)}, u32[]{:S(2)}, u32[]{:S(2)}) %collective-permute-start.1) | collective-permute-done | bytes 1048608 | tf_op jit(solution)/shard_map/ppermute | solution.py:48
  197.4 1.9 fusion.48
  199.3 1.4 fusion.71
  200.7 1.1 copy.61
  (48 shorter events, 0.4 us)
Async XLA Ops:
  8.0 57.1 %copy-start = (bf16[3,256,256]{2,1,0:T(8,128)(2,1)S(1)}, bf16[3,256,256]{2,1,0:T(8,128)(2,1)}, u32[]{:S(2)}) copy-start(bf16[3,256,256]{2,1,0:T(8,128)(2,1)} %param.6) | copy-start | bytes 1179652
  8.0 48.3 %all-gather.6.cloned.1.call-start = ((), (), s32[]{:S(2)}) async-start(), calls=%async_computation.2 | async-start | bytes 2621440 | tf_op jit(solution)/shard_map/all_gather | solution.py:101
  10.2 3.0 %copy-start.8 = (bf16[3,3,128,64]{2,3,1,0:T(8,128)(2,1)S(1)}, bf16[3,3,128,64]{2,3,1,0:T(8,128)(2,1)}, u32[]{:S(2)}) copy-start(bf16[3,3,128,64]{2,3,1,0:T(8,128)(2,1)} %param.5) | copy-start | bytes 442372
  10.2 73.5 %reduce-scatter.5.cloned.1.call-start = ((), (), s32[]{:S(2)}) async-start(), calls=%async_computation.4 | async-start | bytes 3145728
  25.3 78.3 %all-gather.8.cloned.1.call-start = ((), (), s32[]{:S(2)}) async-start(), calls=%async_computation.3 | async-start | bytes 1572864 | tf_op jit(solution)/shard_map/all_gather | solution.py:104
  56.3 23.2 %copy-start.2 = (bf16[256,2,16,128]{3,0,2,1:T(8,128)(2,1)S(1)}, bf16[256,2,16,128]{3,0,2,1:T(8,128)(2,1)}, u32[]{:S(2)}) copy-start(bf16[256,2,16,128]{3,0,2,1:T(8,128)(2,1)} %all-gather.6.cloned.1.call-done) | copy-start | bytes 6291460
  59.3 15.9 %collective-permute-start.2 = (bf16[256,1,16,128]{3,0,2,1:T(8,128)(2,1)}, bf16[256,1,16,128]{3,0,2,1:T(8,128)(2,1)}, u32[]{:S(2)}, u32[]{:S(2)}) collective-permute-start(bf16[256,1,16,128]{3,0,2,1:T(8,128)(2,1)} %get-tuple-element.10), channel_id=1, source_target_pairs={{0,8},{8,16},{16,24},{1,9},{9,17},{17,25},{2,10},{10,18},{18,26},{... | collective-permute-start | bytes 3145736 | tf_op jit(solution)/shard_map/ppermute | solution.py:47
  63.2 16.4 %collective-permute-start.3 = (bf16[256,1,16,128]{3,0,2,1:T(8,128)(2,1)S(1)}, bf16[256,1,16,128]{3,0,2,1:T(8,128)(2,1)}, u32[]{:S(2)}, u32[]{:S(2)}) collective-permute-start(bf16[256,1,16,128]{3,0,2,1:T(8,128)(2,1)S(1)} %get-tuple-element.11), channel_id=1, source_target_pairs={{8,0},{16,8},{24,16},{9,1},{17,9},{25,17},{10,2},{18,10},{26,18},{... | collective-permute-start | bytes 3145736 | tf_op jit(solution)/shard_map/ppermute | solution.py:48
  67.5 14.0 %copy-start.13 = (bf16[3,256,64]{2,1,0:T(8,128)(2,1)S(1)}, bf16[3,256,64]{2,1,0:T(8,128)(2,1)}, u32[]{:S(2)}) copy-start(bf16[3,256,64]{2,1,0:T(8,128)(2,1)} %rev.6) | copy-start | bytes 294916
  83.6 2.4 %copy-start.9 = (bf16[3,3,128,64]{2,3,1,0:T(8,128)(2,1)S(1)}, bf16[3,3,128,64]{2,3,1,0:T(8,128)(2,1)}, u32[]{:S(2)}) copy-start(bf16[3,3,128,64]{2,3,1,0:T(8,128)(2,1)} %param.5) | copy-start | bytes 442372
  83.6 85.3 %all-gather.4.cloned.1.call-start = ((), (), s32[]{:S(2)}) async-start(), calls=%async_computation.1 | async-start | bytes 2621440 | tf_op jit(solution)/shard_map/all_gather | solution.py:98
  105.1 26.5 %collective-permute-start.6 = (bf16[64,2,8,128]{3,2,1,0:T(8,128)(2,1)S(1)}, bf16[64,2,8,128]{3,2,1,0:T(8,128)(2,1)S(1)}, u32[]{:S(2)}, u32[]{:S(2)}) collective-permute-start(bf16[64,2,8,128]{3,2,1,0:T(8,128)(2,1)S(1)} %bitcast.119), channel_id=1, source_target_pairs={{0,3},{1,2},{2,1},{3,0},{4,7},{5,6},{6,5},{7,4},{8,11},{9,10},{10,... | collective-permute-start | bytes 786440 | tf_op jit(solution)/shard_map/ppermute | solution.py:31
  106.5 39.1 %collective-permute-start.5 = (bf16[64,2,8,128]{3,2,1,0:T(8,128)(2,1)S(1)}, bf16[64,2,8,128]{3,2,1,0:T(8,128)(2,1)S(1)}, u32[]{:S(2)}, u32[]{:S(2)}) collective-permute-start(bf16[64,2,8,128]{3,2,1,0:T(8,128)(2,1)S(1)} %bitcast.120), channel_id=1, source_target_pairs={{0,2},{1,3},{2,0},{3,1},{4,6},{5,7},{6,4},{7,5},{8,10},{9,11},{10,... | collective-permute-start | bytes 786440 | tf_op jit(solution)/shard_map/ppermute | solution.py:31
  107.9 37.7 %collective-permute-start.4 = (bf16[64,2,8,128]{3,2,1,0:T(8,128)(2,1)S(1)}, bf16[64,2,8,128]{3,2,1,0:T(8,128)(2,1)S(1)}, u32[]{:S(2)}, u32[]{:S(2)}) collective-permute-start(bf16[64,2,8,128]{3,2,1,0:T(8,128)(2,1)S(1)} %bitcast.121), channel_id=1, source_target_pairs={{0,1},{1,0},{2,3},{3,2},{4,5},{5,4},{6,7},{7,6},{8,9},{9,8},{10,11... | collective-permute-start | bytes 786440 | tf_op jit(solution)/shard_map/ppermute | solution.py:31
  146.5 13.2 %copy-start.3 = (bf16[3,3,256,128]{3,2,1,0:T(8,128)(2,1)S(1)}, bf16[3,3,256,128]{3,2,1,0:T(8,128)(2,1)}, u32[]{:S(2)}) copy-start(bf16[3,3,256,128]{3,2,1,0:T(8,128)(2,1)} %reverse_bitcast_fusion) | copy-start | bytes 1769476
  147.3 14.6 %collective-permute-start.8 = (bf16[256,2,1,128]{0,3,2,1:T(8,128)(2,1)S(1)}, bf16[256,2,1,128]{0,3,2,1:T(8,128)(2,1)S(1)}, u32[]{:S(2)}, u32[]{:S(2)}) collective-permute-start(bf16[256,2,1,128]{0,3,2,1:T(8,128)(2,1)S(1)} %get-tuple-element.31), channel_id=1, source_target_pairs={{1,0},{2,1},{3,2},{5,4},{6,5},{7,6},{9,8},{10,9},{11,10},{13,12},{... | collective-permute-start | bytes 393224 | tf_op jit(solution)/shard_map/ppermute | solution.py:48
  157.8 6.6 %collective-permute-start.7 = (bf16[256,2,1,128]{0,3,2,1:T(8,128)(2,1)S(1)}, bf16[256,2,1,128]{0,3,2,1:T(8,128)(2,1)S(1)}, u32[]{:S(2)}, u32[]{:S(2)}) collective-permute-start(bf16[256,2,1,128]{0,3,2,1:T(8,128)(2,1)S(1)} %get-tuple-element.30), channel_id=1, source_target_pairs={{0,1},{1,2},{2,3},{4,5},{5,6},{6,7},{8,9},{9,10},{10,11},{12,13},{... | collective-permute-start | bytes 393224 | tf_op jit(solution)/shard_map/ppermute | solution.py:47
  161.9 2.4 %copy-start.16 = (bf16[256,2,1,128]{0,3,2,1:T(8,128)(2,1)}, bf16[256,2,1,128]{0,3,2,1:T(8,128)(2,1)S(1)}, u32[]{:S(2)}) copy-start(bf16[256,2,1,128]{0,3,2,1:T(8,128)(2,1)S(1)} %collective-permute-done.8) | copy-start | bytes 393220
  164.4 0.7 copy-start.14
  168.9 14.2 %copy-start.6 = (bf16[256,2,8,128]{0,3,2,1:T(8,128)(2,1)S(1)}, bf16[256,2,8,128]{0,3,2,1:T(8,128)(2,1)}, u32[]{:S(2)}) copy-start(bf16[256,2,8,128]{0,3,2,1:T(8,128)(2,1)} %get-tuple-element.26) | copy-start | bytes 3145732
  168.9 14.2 %copy-start.7 = (bf16[256,2,8,128]{0,3,2,1:T(8,128)(2,1)S(1)}, bf16[256,2,8,128]{0,3,2,1:T(8,128)(2,1)}, u32[]{:S(2)}) copy-start(bf16[256,2,8,128]{0,3,2,1:T(8,128)(2,1)} %get-tuple-element.27) | copy-start | bytes 3145732
  168.9 14.2 %copy-start.12 = (bf16[1,3,256,128]{3,2,1,0:T(8,128)(2,1)S(1)}, bf16[1,3,256,128]{3,2,1,0:T(8,128)(2,1)}, u32[]{:S(2)}) copy-start(bf16[1,3,256,128]{3,2,1,0:T(8,128)(2,1)} %get-tuple-element.38) | copy-start | bytes 589828
  172.2 20.8 %collective-permute-start = (bf16[256,1,16,128]{3,0,2,1:T(8,128)(2,1)}, bf16[256,1,16,128]{3,0,2,1:T(8,128)(2,1)}, u32[]{:S(2)}, u32[]{:S(2)}) collective-permute-start(bf16[256,1,16,128]{3,0,2,1:T(8,128)(2,1)} %get-tuple-element.14), channel_id=1, source_target_pairs={{0,8},{8,16},{16,24},{1,9},{9,17},{17,25},{2,10},{10,18},{18,26},{... | collective-permute-start | bytes 3145736 | tf_op jit(solution)/shard_map/ppermute | solution.py:47
  181.0 16.4 %collective-permute-start.1 = (bf16[256,1,16,128]{3,0,2,1:T(8,128)(2,1)}, bf16[256,1,16,128]{3,0,2,1:T(8,128)(2,1)}, u32[]{:S(2)}, u32[]{:S(2)}) collective-permute-start(bf16[256,1,16,128]{3,0,2,1:T(8,128)(2,1)} %get-tuple-element.15), channel_id=1, source_target_pairs={{8,0},{16,8},{24,16},{9,1},{17,9},{25,17},{10,2},{18,10},{26,18},{... | collective-permute-start | bytes 3145736 | tf_op jit(solution)/shard_map/ppermute | solution.py:48
  183.1 1.2 copy-start.11
  183.1 1.2 copy-start.17
  184.4 1.2 copy-start.4
  184.4 1.5 copy-start.5
  184.4 1.5 copy-start.10
  184.4 1.6 copy-start.15
  185.9 11.5 %copy-start.1 = (bf16[256,2,16,128]{3,0,2,1:T(8,128)(2,1)S(1)}, bf16[256,2,16,128]{3,0,2,1:T(8,128)(2,1)}, u32[]{:S(2)}) copy-start(bf16[256,2,16,128]{3,0,2,1:T(8,128)(2,1)} %all-gather.4.cloned.1.call-done) | copy-start | bytes 6291460
Sparse Core Ops, SparseCore 0:
  11.1 45.2 all-gather.5
Sparse Core Ops, SparseCore 1:
  25.4 32.8 reduce-scatter.4
  83.7 19.9 all-gather.7
  105.8 58.9 all-gather.3
